TPU v7x, 128 devices: a whole 4x4x4 slice. The times are simulated.
128 devices in a mesh: row: 8 (over x, core), col: 16 (over z, y).
Axes of the slice: x: 4, y: 4, z: 4, core: 2. Of those that a mesh axis runs over, the one named last changes fastest.
Arguments:
- left_factor: float32 [23, 8, 128, 16, 16, 128], P(None, 'row', None, None, 'col'), may hold values from -5 to 5
- pick_site: int32 [23, 8, 128], P(None, 'row'), may hold values from 0 to 131071
- noise: float32 [23, 8, 128], P(None, 'row'), may hold values from 2 to 5
Outputs:
- panels: float32 [8, 16, 184, 2, 128], P('row', 'col')
All inputs are finite; a program needn't handle non-finite values.
Results may differ from a plain program's by a relative error of at most 0.000064.
Values sent between devices are 32-bit elements; how exact they have to be, the bound alone decides.
No kernel may reach another device: no remote copies, remote signals or barrier semaphores. Data moves between devices by JAX's collectives and lax.ppermute only.
A program may use at most 128 MiB of HBM per device.

v0:
```python
import jax
import jax.numpy as jnp
from jax import lax
from jax.sharding import PartitionSpec as P

GRID_Y = 64
GRID_Z = 32
LATERAL = 24.0
VERTICAL = 6.0


def spread(block, axis, owner):
    block = jnp.where(lax.axis_index(axis) == owner, block, jnp.zeros_like(block))
    return lax.psum(block, axis)


def site_coords(site_ids):
    coord_x = site_ids // (GRID_Y * GRID_Z)
    coord_y = site_ids // GRID_Z % GRID_Y
    coord_z = site_ids % GRID_Z
    return jnp.stack([coord_x, coord_y, coord_z]).astype(jnp.float32)


def matern(row_coords, col_coords):
    lengths = (LATERAL, LATERAL, VERTICAL)
    squared = jnp.zeros((row_coords.shape[1], col_coords.shape[1]), jnp.float32)
    for dim_index in range(3):
        difference = (row_coords[dim_index][:, None] - col_coords[dim_index][None, :]) / lengths[
            dim_index
        ]
        squared = squared + difference * difference
    radius = jnp.sqrt(3.0 * squared)
    return (1.0 + radius) * jnp.exp(-radius)


def times_transposed(left_mat, right_mat):
    return lax.dot_general(
        left_mat,
        right_mat,
        (((1,), (1,)), ((), ())),
        precision=lax.Precision.HIGHEST,
        preferred_element_type=jnp.float32,
    )


def lower_inverse(square):
    factor = jnp.linalg.cholesky(square)
    return jax.scipy.linalg.solve_triangular(
        factor, jnp.eye(square.shape[0], dtype=jnp.float32), lower=True
    )


def body(left_factor, pick_site, noise):
    row_blocks, _, block_width, col_blocks, _, _ = left_factor.shape
    col_count = lax.axis_size("col")
    row_share = row_blocks * block_width // col_count
    row_index = lax.axis_index("row")
    col_index = lax.axis_index("col")
    local_rows = left_factor.reshape(row_blocks * block_width, col_blocks * block_width)
    site_flat = pick_site.reshape(row_blocks * block_width)
    noise_flat = noise.reshape(row_blocks * block_width)
    offset = col_index * row_share
    my_coords = site_coords(lax.dynamic_slice_in_dim(site_flat, offset, row_share))
    my_noise = lax.dynamic_slice_in_dim(noise_flat, offset, row_share)
    head_rows = local_rows[:block_width]
    head_coords = site_coords(site_flat[:block_width])
    first_owner = (row_index == 0) & (col_index == 0)
    second_owner = (row_index == 1) & (col_index == 0)
    own_diag = jnp.diag(my_noise[:block_width])

    def terms_for(lead_rows):
        return times_transposed(local_rows, lead_rows)

    first_head, first_coords = (spread(head_rows, "row", 0), spread(head_coords, "row", 0))
    first_sums = lax.psum_scatter(terms_for(first_head), "col", scatter_dimension=0, tiled=True)
    second_head, second_coords = (spread(head_rows, "row", 1), spread(head_coords, "row", 1))
    second_sums = lax.psum_scatter(terms_for(second_head), "col", scatter_dimension=0, tiled=True)
    first_cov = matern(my_coords, first_coords) - first_sums
    first_cov = first_cov.at[:block_width].add(jnp.where(first_owner, own_diag, 0.0))
    first_diag = spread(first_cov[:block_width], ("row", "col"), 0)
    first_panel = times_transposed(first_cov, lower_inverse(first_diag))
    own_cross = first_panel[:block_width]
    second_base = matern(my_coords, second_coords) - second_sums
    second_nugget = jnp.where(second_owner, own_diag, 0.0)
    cross_rows = spread(own_cross, ("row", "col"), col_count)
    second_cov = (
        (second_base - times_transposed(first_panel, cross_rows))
        .at[:block_width]
        .add(second_nugget)
    )
    second_diag = spread(second_cov[:block_width], ("row", "col"), col_count)
    second_panel = times_transposed(second_cov, lower_inverse(second_diag))
    stacked = jnp.stack([first_panel, second_panel], axis=1)
    return stacked.reshape(1, 1, row_share, 2, block_width)


def solution(mesh):
    placed = (P(None, "row", None, None, "col", None), P(None, "row", None), P(None, "row", None))
    return jax.shard_map(
        body,
        mesh=mesh,
        in_specs=placed,
        out_specs=P("row", "col", None, None, None),
        check_vma=False,
    )
```

profile of v0, /device:TPU:1, one launch (start us, length us, event | category | flops | bytes accessed | tf_op | source)
XLA Modules:
  0.0 742.1 jit_solution(13601761181299983725)
XLA Ops:
  6.5 0.0 all-reduce.19.cloned.1.call-start
  6.5 6.9 fusion.13
  13.5 2.3 copy_bitcast_fusion
  15.8 0.0 all-reduce.19.cloned.1.call-update
  15.8 0.0 all-reduce.17.cloned.1.call-start
  15.8 67.1 %all-reduce.19.cloned.1.call-done = (f32[128,2048]{1,0:T(8,128)}, f32[128,2048]{1,0:T(8,128)}) async-done(((f32[128,2048]{1,0:T(8,128)}, f32[128,2048]{1,0:T(8,128)}), (f32[128,2048]{1,0:T(8,128)}, f32[128,2048]{1,0:T(8,128)})) %all-reduce.19.cloned.1.call-update) | async-done | bytes 2097168 | tf_op jit(solution)/shard_map/psum | solution.py:14
  83.0 0.0 copy-start
  83.0 0.0 copy-start.1
  83.0 0.0 copy-start.2
  83.0 0.0 copy-start.3
  83.0 40.9 %fusion.6 = f32[2944,128]{0,1:T(8,128)} fusion(f32[128,2048]{1,0:T(8,128)} %get-tuple-element.37, f32[368,8,16,128]{3,2,1,0:T(8,128)} %bitcast.102), kind=kOutput, calls=%fused_computation.6 | convolution fusion | flops 9261023232 | bytes 26673152 | tf_op jit(solution)/shard_map/dot_general | solution.py:37
  123.9 0.0 copy-done
  123.9 40.5 %fusion.9 = f32[2944,128]{0,1:T(8,128)} fusion(f32[128,2048]{1,0:T(8,128)S(1)} %copy-done, f32[368,8,16,128]{3,2,1,0:T(8,128)} %bitcast.103), kind=kOutput, calls=%fused_computation.7 | convolution fusion | flops 9261023232 | bytes 26673152 | tf_op jit(solution)/shard_map/dot_general | solution.py:37
  164.4 0.0 all-reduce.17.cloned.1.call-update
  164.5 0.0 all-reduce.11.cloned.1.call-start
  164.5 0.0 copy-done.1
  164.6 0.0 copy-done.2
  164.6 0.1 dynamic_slice.7
  164.7 0.0 copy-done.3
  164.7 0.6 dynamic-slice.16
  166.0 14.3 %all-reduce.3 = (f32[3,128]{1,0:T(4,128)S(1)}, f32[3,128]{1,0:T(4,128)S(1)}) all-reduce(f32[3,128]{1,0:T(4,128)S(1)} %get-tuple-element.59, f32[3,128]{1,0:T(4,128)S(1)} %get-tuple-element.58), channel_id=1, replica_groups=mesh['row'=8,'col'=16] {'row'}, use_global_device_ids=true, to_apply=%region_0.1 | all-reduce | flops 768 | bytes 6144 | tf_op jit(solution)/shard_map/psum | solution.py:14
  180.3 0.1 and_select_fusion.7
  180.4 80.7 %all-reduce.17.cloned.1.call-done = (f32[2944,128]{0,1:T(8,128)}, f32[2944,128]{0,1:T(8,128)}) async-done(((f32[2944,128]{0,1:T(8,128)}, f32[2944,128]{0,1:T(8,128)}), (f32[2944,128]{0,1:T(8,128)}, f32[2944,128]{0,1:T(8,128)})) %all-reduce.17.cloned.1.call-update) | async-done | bytes 3014672
  261.1 1.1 dynamic-slice_subtract_fusion.1
  262.3 0.7 fusion.28
  262.9 0.0 all-reduce.11.cloned.1.call-update
  263.0 0.0 all-reduce.13.cloned.1.call-start
  263.0 142.0 %all-reduce.11.cloned.1.call-done = f32[128,128]{0,1:T(8,128)} async-done(((f32[128,128]{0,1:T(8,128)}), f32[128,128]{0,1:T(8,128)}) %all-reduce.11.cloned.1.call-update) | async-done | bytes 65552 | tf_op jit(solution)/shard_map/psum | solution.py:14
  405.0 0.9 copy.15
  405.9 0.9 fusion.25
  406.8 11.7 %cholesky.44 = f32[128,128]{1,0:T(8,128)S(1)} custom-call(f32[128,128]{1,0:T(8,128)S(1)} %fusion.25), custom_call_target="Cholesky" | custom-call | tf_op jit(solution)/shard_map/jit(cholesky)/cholesky | solution.py:47
  418.5 0.6 compare_reduce_fusion.1
  419.1 0.7 fusion.18
  419.8 9.8 %custom-call.6 = f32[1,128,128]{1,2,0:T(8,128)S(1)} custom-call(f32[1,128,128]{2,1,0:T(8,128)S(1)} %fusion.18), custom_call_target="InvertDiagBlocksLowerTriangular" | custom-call | tf_op jit(solution)/shard_map/jit(_solve_triangular)/triangular_solve | solution.py:48
  429.6 0.3 fusion.16
  429.9 0.4 fusion.35
  430.4 0.1 copy.26
  430.4 0.6 broadcast_select_fusion.2
  431.1 0.0 all-reduce.13.cloned.1.call-update
  431.1 0.3 all-reduce.15.cloned.1.call-start
  431.4 136.5 %all-reduce.13.cloned.1.call-done = f32[128,128]{0,1:T(8,128)} async-done(((f32[128,128]{0,1:T(8,128)}), f32[128,128]{0,1:T(8,128)}) %all-reduce.13.cloned.1.call-update) | async-done | bytes 65552 | tf_op jit(solution)/shard_map/psum | solution.py:14
  567.9 1.3 convolution_subtract_fusion
  569.2 0.7 fusion.26
  569.9 0.0 all-reduce.15.cloned.1.call-update
  569.9 139.2 %all-reduce.15.cloned.1.call-done = f32[128,128]{0,1:T(8,128)} async-done(((f32[128,128]{0,1:T(8,128)}), f32[128,128]{0,1:T(8,128)}) %all-reduce.15.cloned.1.call-update) | async-done | bytes 65552 | tf_op jit(solution)/shard_map/psum | solution.py:14
  709.1 0.9 copy.19
  710.1 0.9 fusion.23
  710.9 11.7 %cholesky.55 = f32[128,128]{1,0:T(8,128)S(1)} custom-call(f32[128,128]{1,0:T(8,128)S(1)} %fusion.23), custom_call_target="Cholesky" | custom-call | tf_op jit(solution)/shard_map/jit(cholesky)/cholesky | solution.py:47
  722.7 0.6 compare_reduce_fusion
  723.3 0.7 fusion.19
  724.0 9.8 %custom-call.7 = f32[1,128,128]{1,2,0:T(8,128)S(1)} custom-call(f32[1,128,128]{2,1,0:T(8,128)S(1)} %fusion.19), custom_call_target="InvertDiagBlocksLowerTriangular" | custom-call | tf_op jit(solution)/shard_map/jit(_solve_triangular)/triangular_solve | solution.py:48
  733.8 0.3 fusion.14
  734.1 0.4 convolution_bitcast_fusion
  734.5 0.8 copy.20
  (13 shorter events, 0.2 us)
Async XLA Ops:
  6.5 76.4 %all-reduce.19.cloned.1.call-start = ((), (), s32[]{:S(2)}) async-start(), calls=%async_computation.4 | async-start | bytes 4194304 | tf_op jit(solution)/shard_map/psum | solution.py:14
  15.8 245.3 %all-reduce.17.cloned.1.call-start = ((), (), s32[]{:S(2)}) async-start(), calls=%async_computation.3 | async-start | bytes 6029312
  83.0 40.9 %copy-start = (f32[128,2048]{1,0:T(8,128)S(1)}, f32[128,2048]{1,0:T(8,128)}, u32[]{:S(2)}) copy-start(f32[128,2048]{1,0:T(8,128)} %get-tuple-element.38) | copy-start | bytes 3145732
  83.0 81.6 %copy-start.1 = (s32[23,1,128]{2,1,0:T(1,128)S(1)}, s32[23,1,128]{2,1,0:T(1,128)}, u32[]{:S(2)}) copy-start(s32[23,1,128]{2,1,0:T(1,128)} %param.11) | copy-start | bytes 35332
  83.0 81.6 %copy-start.2 = (f32[23,1,128]{2,1,0:T(1,128)S(1)}, f32[23,1,128]{2,1,0:T(1,128)}, u32[]{:S(2)}) copy-start(f32[23,1,128]{2,1,0:T(1,128)} %param.12) | copy-start | bytes 35332
  83.0 81.7 %copy-start.3 = (u32[128]{0:T(128)S(1)}, u32[128]{0:T(128)}, u32[]{:S(2)}) copy-start(u32[128]{0:T(128)} %constant.200) | copy-start | bytes 1540
  164.5 240.5 %all-reduce.11.cloned.1.call-start = ((), (), s32[]{:S(2)}) async-start(), calls=%async_computation | async-start | bytes 131072 | tf_op jit(solution)/shard_map/psum | solution.py:14
  263.0 305.0 %all-reduce.13.cloned.1.call-start = ((), (), s32[]{:S(2)}) async-start(), calls=%async_computation.1 | async-start | bytes 131072 | tf_op jit(solution)/shard_map/psum | solution.py:14
  431.1 278.0 %all-reduce.15.cloned.1.call-start = ((), (), s32[]{:S(2)}) async-start(), calls=%async_computation.2 | async-start | bytes 131072 | tf_op jit(solution)/shard_map/psum | solution.py:14
Sparse Core Ops, SparseCore 0:
  15.9 67.0 all-reduce.18
  164.6 96.5 all-reduce.16
  265.9 139.0 all-reduce.10
  431.2 136.6 all-reduce.12
  572.5 136.6 all-reduce.14
where the time goes:
time: 746 us; the launch traced here: 742 us
  waiting for transfers between devices  566 us (76%)
  matrix products  84.2 us (11%)
  other arithmetic  57.7 us (8%)
  blocking collectives  14.3 us (2%)
  between operations  14.3 us (2%)
    psum x4, waiting for transfers between devices, spread(): return lax.psum(block, axis)  485 us
    dot_general x5, matrix products, times_transposed(): lax.dot_general(left_mat, right_mat, (((1,), (1,)), ((), ())), precision=...  83.6 us
    unnamed x6, waiting for transfers between devices  80.8 us
    another operation x6, other arithmetic, lower_inverse(): factor = jnp.linalg.cholesky(square)  24.8 us
    another operation x4, other arithmetic, lower_inverse(): jax.scipy.linalg.solve_triangular(factor, jnp.eye(square.shape[0], dtype=...  20.9 us
  transfers between devices with their start and end apart: 5, of which 5 were waited for; matrix products, arithmetic and copies ran while one was open for 0% of the time, Pallas kernels for 0%

commit v1 on v0

--- a/solution.py
+++ b/solution.py
@@ -11,7 +11,7 @@
 
 def spread(block, axis, owner):
     block = jnp.where(lax.axis_index(axis) == owner, block, jnp.zeros_like(block))
-    return lax.psum(block, axis)
+    return jnp.sum(lax.all_gather(block, axis), axis=0)
 
 
 def site_coords(site_ids):

time: 746 us -> 539 us (0.72)
  waiting for transfers between devices: 566 us -> 333 us
  other arithmetic: 57.7 us -> 74.8 us
  blocking collectives: 14.3 us -> 23 us
    psum x4 -> x0, waiting for transfers between devices: 485 us -> none  [spread(): return lax.psum(block, axis)]
    all_gather x0 -> x5, waiting for transfers between devices: none -> 251 us  [spread(): return jnp.sum(lax.all_gather(block, axis), axis=0)]
    all_gather x0 -> x2, blocking collectives: none -> 23 us  [spread(): return jnp.sum(lax.all_gather(block, axis), axis=0)]
    reduce_sum x0 -> x6, other arithmetic: none -> 16 us  [spread(): return jnp.sum(lax.all_gather(block, axis), axis=0)]
    psum x1 -> x0, blocking collectives: 14.3 us -> none  [spread(): return lax.psum(block, axis)]
    unnamed x6 -> x7, waiting for transfers between devices: 80.8 us -> 81.9 us
  transfers between devices with their start and end apart: 5 -> 6, of which waited for: 5 -> 6; matrix products, arithmetic and copies ran while one was open for 0% -> 9% of each run, Pallas kernels for 0% -> 0%
where the time goes in v1:
time: 539 us; the launch traced here: 535 us
  waiting for transfers between devices  333 us (62%)
  matrix products  82.6 us (15%)
  other arithmetic  74.8 us (14%)
  blocking collectives  23 us (4%)
  between operations  14.6 us (3%)
  local copies, waits for them, and re-layouts  6.22 us (1%)
    all_gather x5, waiting for transfers between devices, spread(): return jnp.sum(lax.all_gather(block, axis), axis=0)  251 us
    dot_general x5, matrix products, times_transposed(): lax.dot_general(left_mat, right_mat, (((1,), (1,)), ((), ())), precision=...  82 us
    unnamed x7, waiting for transfers between devices  81.9 us
    another operation x6, other arithmetic, lower_inverse(): factor = jnp.linalg.cholesky(square)  24.8 us
    all_gather x2, blocking collectives, spread(): return jnp.sum(lax.all_gather(block, axis), axis=0)  23 us
    another operation x4, other arithmetic, lower_inverse(): jax.scipy.linalg.solve_triangular(factor, jnp.eye(square.shape[0], dtype=...  20.9 us
    reduce_sum x6, other arithmetic, spread(): return jnp.sum(lax.all_gather(block, axis), axis=0)  16 us
  transfers between devices with their start and end apart: 6, of which 6 were waited for; matrix products, arithmetic and copies ran while one was open for 9% of the time, Pallas kernels for 0%

profile of v1, /device:TPU:1, one launch (start us, length us, event | category | flops | bytes accessed | tf_op | source)
XLA Modules:
  0.0 534.7 jit_solution(1053083655918033256)
XLA Ops:
  6.5 0.0 all-gather.9.cloned.1.call-start
  6.5 6.8 %fusion.13 = (f32[128,16,128]{2,1,0:T(8,128)S(1)}, f32[128,16,128]{2,1,0:T(8,128)S(1)}) fusion(pred[]{:T(512)S(6)} %eq.41, f32[23,1,128,16,1,128]{5,4,3,2,1,0:T(1,128)} %param.10, pred[]{:T(512)S(6)} %eq.37), kind=kLoop, calls=%fused_computation.13 | loop fusion | flops 524288 | bytes 3145730 | tf_op jit(solution)/shard_map/jit(_where)/select_n | solution.py:13
  13.3 1.2 select_n.172
  14.5 0.0 all-gather.9.cloned.1.call-update
  14.6 0.0 all-gather.11.cloned.1.call-start
  14.6 1.2 select_n.182
  15.8 0.0 all-gather.11.cloned.1.call-update
  15.8 0.0 all-reduce.5.cloned.1.call-start
  15.8 52.1 %all-gather.9.cloned.1.call-done = f32[8,128,2048]{2,1,0:T(8,128)} async-done(((f32[1,128,2048]{2,1,0:T(8,128)}), f32[8,128,2048]{2,1,0:T(8,128)}) %all-gather.9.cloned.1.call-update) | async-done | bytes 8388624 | tf_op jit(solution)/shard_map/all_gather | solution.py:14
  67.9 4.2 reduce_sum.64
  72.1 40.3 %fusion.6 = f32[2944,128]{0,1:T(8,128)} fusion(f32[128,2048]{1,0:T(8,128)S(1)} %reduce_sum.64, f32[368,8,16,128]{3,2,1,0:T(8,128)} %bitcast.76), kind=kOutput, calls=%fused_computation.6 | convolution fusion | flops 9261023232 | bytes 26673152 | tf_op jit(solution)/shard_map/dot_general | solution.py:37
  112.5 7.0 %all-gather.11.cloned.1.call-done = f32[8,128,2048]{2,1,0:T(8,128)} async-done(((f32[1,128,2048]{2,1,0:T(8,128)}), f32[8,128,2048]{2,1,0:T(8,128)}) %all-gather.11.cloned.1.call-update) | async-done | bytes 8388624 | tf_op jit(solution)/shard_map/all_gather | solution.py:14
  119.5 4.2 reduce_sum.67
  123.7 0.0 copy-start
  123.7 0.0 copy-start.1
  123.7 0.0 copy-start.2
  123.7 40.7 %fusion.9 = f32[2944,128]{0,1:T(8,128)} fusion(f32[128,2048]{1,0:T(8,128)S(1)} %reduce_sum.67, f32[368,8,16,128]{3,2,1,0:T(8,128)} %bitcast.77), kind=kOutput, calls=%fused_computation.7 | convolution fusion | flops 9261023232 | bytes 26673152 | tf_op jit(solution)/shard_map/dot_general | solution.py:37
  164.4 0.0 all-reduce.5.cloned.1.call-update
  164.5 0.0 all-gather.13.cloned.1.call-start
  164.5 0.0 copy-done
  164.6 11.4 %all_gather.34 = f32[8,3,128]{2,1,0:T(4,128)S(1)} all-gather(f32[1,3,128]{2,1,0:T(4,128)S(1)} %get-tuple-element.55), channel_id=1, replica_groups=mesh['row'=8,'col'=16] {'row'}, dimensions={0}, use_global_device_ids=true | all-gather | bytes 13824 | tf_op jit(solution)/shard_map/all_gather | solution.py:14
  176.0 0.0 copy-done.1
  176.1 0.1 dynamic_slice.7
  176.2 0.0 copy-done.2
  176.2 0.6 dynamic-slice.16
  177.4 0.1 and_select_fusion.7
  177.5 81.8 %all-reduce.5.cloned.1.call-done = (f32[2944,128]{0,1:T(8,128)}, f32[2944,128]{0,1:T(8,128)}) async-done(((f32[2944,128]{0,1:T(8,128)}, f32[2944,128]{0,1:T(8,128)}), (f32[2944,128]{0,1:T(8,128)}, f32[2944,128]{0,1:T(8,128)})) %all-reduce.5.cloned.1.call-update) | async-done | bytes 3014672
  259.3 1.0 constant_dynamic-slice_fusion.1
  260.4 0.1 copy.15
  260.5 0.2 multiply_subtract_fusion
  260.6 0.7 fusion.28
  261.4 0.0 all-gather.13.cloned.1.call-update
  261.4 0.0 all-gather.15.cloned.1.call-start
  261.5 70.3 %all-gather.13.cloned.1.call-done = f32[16384,128]{1,0:T(8,128)} async-done(((f32[128,128]{1,0:T(8,128)}), f32[16384,128]{1,0:T(8,128)}) %all-gather.13.cloned.1.call-update) | async-done | bytes 8388624 | tf_op jit(solution)/shard_map/all_gather | solution.py:14
  331.7 3.8 reduce_sum.65
  335.5 0.1 copy.16
  335.7 11.7 %cholesky.44 = f32[128,128]{1,0:T(8,128)S(1)} custom-call(f32[128,128]{1,0:T(8,128)S(1)} %fusion.25), custom_call_target="Cholesky" | custom-call | tf_op jit(solution)/shard_map/jit(cholesky)/cholesky | solution.py:47
  347.4 0.6 compare_reduce_fusion.1
  348.0 0.7 fusion.18
  348.7 9.8 %custom-call.6 = f32[1,128,128]{1,2,0:T(8,128)S(1)} custom-call(f32[1,128,128]{2,1,0:T(8,128)S(1)} %fusion.18), custom_call_target="InvertDiagBlocksLowerTriangular" | custom-call | tf_op jit(solution)/shard_map/jit(_solve_triangular)/triangular_solve | solution.py:48
  358.5 0.3 fusion.16
  358.8 0.3 fusion.35
  359.1 0.6 slice_select_fusion
  359.8 0.0 all-gather.15.cloned.1.call-update
  359.8 0.0 all-gather.17.cloned.1.call-start
  359.9 11.6 %all_gather.38 = f32[8,3,128]{2,1,0:T(4,128)S(1)} all-gather(f32[1,3,128]{2,1,0:T(4,128)S(1)} %get-tuple-element.54), channel_id=1, replica_groups=mesh['row'=8,'col'=16] {'row'}, dimensions={0}, use_global_device_ids=true | all-gather | bytes 13824 | tf_op jit(solution)/shard_map/all_gather | solution.py:14
  371.5 1.0 constant_dynamic-slice_fusion
  372.5 0.1 copy.17
  372.6 54.5 %all-gather.15.cloned.1.call-done = f32[16384,128]{1,0:T(8,128)} async-done(((f32[128,128]{1,0:T(8,128)}), f32[16384,128]{1,0:T(8,128)}) %all-gather.15.cloned.1.call-update) | async-done | bytes 8388624 | tf_op jit(solution)/shard_map/all_gather | solution.py:14
  427.2 3.8 reduce_sum.68
  431.0 0.3 convolution_subtract_fusion
  431.3 0.7 fusion.26
  432.0 0.0 all-gather.17.cloned.1.call-update
  432.0 67.4 %all-gather.17.cloned.1.call-done = f32[16384,128]{1,0:T(8,128)} async-done(((f32[128,128]{1,0:T(8,128)}), f32[16384,128]{1,0:T(8,128)}) %all-gather.17.cloned.1.call-update) | async-done | bytes 8388624 | tf_op jit(solution)/shard_map/all_gather | solution.py:14
  499.4 3.8 reduce_sum.69
  503.2 0.1 copy.19
  503.3 11.7 %cholesky.55 = f32[128,128]{1,0:T(8,128)S(1)} custom-call(f32[128,128]{1,0:T(8,128)S(1)} %fusion.23), custom_call_target="Cholesky" | custom-call | tf_op jit(solution)/shard_map/jit(cholesky)/cholesky | solution.py:47
  515.1 0.6 compare_reduce_fusion
  515.7 0.7 fusion.19
  516.4 9.8 %custom-call.7 = f32[1,128,128]{1,2,0:T(8,128)S(1)} custom-call(f32[1,128,128]{2,1,0:T(8,128)S(1)} %fusion.19), custom_call_target="InvertDiagBlocksLowerTriangular" | custom-call | tf_op jit(solution)/shard_map/jit(_solve_triangular)/triangular_solve | solution.py:48
  526.2 0.3 fusion.14
  526.5 0.3 convolution_bitcast_fusion
  526.8 0.8 copy.20
  (16 shorter events, 0.3 us)
Async XLA Ops:
  6.5 61.4 %all-gather.9.cloned.1.call-start = ((), (), s32[]{:S(2)}) async-start(), calls=%async_computation | async-start | bytes 9437184 | tf_op jit(solution)/shard_map/all_gather | solution.py:14
  14.6 104.9 %all-gather.11.cloned.1.call-start = ((), (), s32[]{:S(2)}) async-start(), calls=%async_computation.1 | async-start | bytes 9437184 | tf_op jit(solution)/shard_map/all_gather | solution.py:14
  15.8 243.6 %all-reduce.5.cloned.1.call-start = ((), (), s32[]{:S(2)}) async-start(), calls=%async_computation.5 | async-start | bytes 6029312
  123.7 40.8 %copy-start = (s32[23,1,128]{2,1,0:T(1,128)S(1)}, s32[23,1,128]{2,1,0:T(1,128)}, u32[]{:S(2)}) copy-start(s32[23,1,128]{2,1,0:T(1,128)} %param.11) | copy-start | bytes 35332
  123.7 52.3 %copy-start.1 = (f32[23,1,128]{2,1,0:T(1,128)S(1)}, f32[23,1,128]{2,1,0:T(1,128)}, u32[]{:S(2)}) copy-start(f32[23,1,128]{2,1,0:T(1,128)} %param.12) | copy-start | bytes 35332
  123.7 52.5 %copy-start.2 = (u32[128]{0:T(128)S(1)}, u32[128]{0:T(128)}, u32[]{:S(2)}) copy-start(u32[128]{0:T(128)} %constant.200) | copy-start | bytes 1540
  164.5 167.3 %all-gather.13.cloned.1.call-start = ((), (), s32[]{:S(2)}) async-start(), calls=%async_computation.2 | async-start | bytes 8454144 | tf_op jit(solution)/shard_map/all_gather | solution.py:14
  261.4 165.8 %all-gather.15.cloned.1.call-start = ((), (), s32[]{:S(2)}) async-start(), calls=%async_computation.3 | async-start | bytes 8454144 | tf_op jit(solution)/shard_map/all_gather | solution.py:14
  359.8 139.6 %all-gather.17.cloned.1.call-start = ((), (), s32[]{:S(2)}) async-start(), calls=%async_computation.4 | async-start | bytes 8454144 | tf_op jit(solution)/shard_map/all_gather | solution.py:14
Sparse Core Ops, SparseCore 0:
  14.7 53.2 all-gather.8
  69.6 49.7 all-gather.10
  164.6 94.7 all-reduce.4
  262.3 69.3 all-gather.12
  359.9 67.1 all-gather.14
  432.2 67.1 all-gather.16
